TPU v7x, 256 devices: a whole 4x4x8 slice. The times are simulated.
256 devices in a mesh: space: 64 (over y, z, core), pa: 2 (over x_lo), pb: 2 (over x_hi).
Axes of the slice: x: 4 (x_hi: 2, x_lo: 2; x = x_hi * 2 + x_lo), y: 4, z: 8, core: 2. Of those that a mesh axis runs over, the one named last changes fastest.
Arguments:
- field: float32 [8192, 16, 16, 16, 16], P('space', 'pa', None, 'pb'), may hold values from -6 to 6
- g_first: float32 [16, 128], P('pa'), may hold values from -1.5 to 1.5
- g_second: float32 [16, 128], replicated, may hold values from -1.5 to 1.5
- g_third: float32 [16, 128], P('pb'), may hold values from -1.5 to 1.5
- g_fourth: float32 [16, 128], replicated, may hold values from -1.5 to 1.5
- h_second: float32 [16, 128], replicated, may hold values from -1.5 to 1.5
- h_third: float32 [16, 128], P('pb'), may hold values from -1.5 to 1.5
- h_fourth: float32 [16, 128], replicated, may hold values from -1.5 to 1.5
Outputs:
- basis: float32 [8192, 128], P('space')
- core: float32 [128, 16, 16, 16, 16], P('space', 'pa', None, 'pb')
- next_sketch: float32 [128, 16, 128], P('space', 'pa')
All inputs are finite; a program needn't handle non-finite values.
Results may differ from a plain program's by a relative error of at most 0.00011.
Values sent between devices are 32-bit elements; how exact they have to be, the bound alone decides.
No kernel may reach another device: no remote copies, remote signals or barrier semaphores. Data moves between devices by JAX's collectives and lax.ppermute only.
A program may use at most 128 MiB of HBM per device.

v0:
```python
import jax
import jax.numpy as jnp
from jax import lax
from jax.sharding import PartitionSpec as P

MODE = 16
RANK = 128


def body(field, g_first, g_second, g_third, g_fourth, h_second, h_third, h_fourth):
    highest = lax.Precision.HIGHEST
    rows = field.shape[0]
    first_loc = field.shape[1]
    third_loc = field.shape[3]
    width = first_loc * MODE * third_loc * MODE
    flat = field.reshape(rows, width)
    omega = (
        g_first[:, None, None, None, :]
        * g_second[None, :, None, None, :]
        * g_third[None, None, :, None, :]
        * g_fourth[None, None, None, :, :]
    ).reshape(width, RANK)
    partial_sketch = jnp.dot(flat, omega, precision=highest, preferred_element_type=jnp.float32)
    sketch = lax.psum(partial_sketch, ("pa", "pb"))
    gram = lax.psum(
        jnp.dot(sketch.T, sketch, precision=highest, preferred_element_type=jnp.float32), "space"
    )
    lower = jnp.linalg.cholesky(gram)
    basis = lax.linalg.triangular_solve(
        lower, sketch, left_side=False, lower=True, transpose_a=True
    )
    core_flat = lax.psum_scatter(
        lax.dot_general(
            basis,
            flat,
            (((0,), (0,)), ((), ())),
            precision=highest,
            preferred_element_type=jnp.float32,
        ),
        "space",
        scatter_dimension=0,
        tiled=True,
    )
    own_rank = core_flat.shape[0]
    psi = (
        h_second[:, None, None, :] * h_third[None, :, None, :] * h_fourth[None, None, :, :]
    ).reshape(MODE * third_loc * MODE, RANK)
    partial_next = jnp.dot(
        core_flat.reshape(own_rank * first_loc, MODE * third_loc * MODE),
        psi,
        precision=highest,
        preferred_element_type=jnp.float32,
    )
    next_sketch = lax.psum(partial_next, "pb")
    core = core_flat.reshape(own_rank, first_loc, MODE, third_loc, MODE)
    return (basis, core, next_sketch.reshape(own_rank, first_loc, RANK))


def solution(mesh):
    placed = (
        P("space", "pa", None, "pb", None),
        P("pa", None),
        P(),
        P("pb", None),
        P(),
        P(),
        P("pb", None),
        P(),
    )
    return jax.shard_map(
        body,
        mesh=mesh,
        in_specs=placed,
        out_specs=(P("space", None), P("space", "pa", None, "pb", None), P("space", "pa", None)),
        check_vma=False,
    )
```

profile of v0, /device:TPU:2, one launch (start us, length us, event | category | flops | bytes accessed | tf_op | source)
XLA Modules:
  0.0 507.3 jit_solution(7857300615730254369)
XLA Ops:
  7.2 0.0 all-reduce.5.cloned.1.call-start
  7.2 0.7 broadcast_multiply_fusion.3
  7.9 0.7 broadcast_multiply_fusion.1
  8.6 16.7 %fusion.4 = f32[128,128]{0,1:T(8,128)} fusion(f32[128,8,16,8,16]{0,4,3,2,1:T(8,128)} %param.8, f32[16,128]{1,0:T(8,128)} %param.12, f32[8,16,8,128]{3,2,1,0:T(8,128)S(1)} %broadcast_multiply_fusion.1), kind=kOutput, calls=%fused_computation.4 | convolution fusion | flops 3223322624 | bytes 8986624 | tf_op jit(solution)/shard_map/dot_general | solution.py:23
  25.4 0.0 all-reduce.5.cloned.1.call-update
  25.4 0.0 all-reduce.7.cloned.1.call-start
  25.4 48.2 %all-reduce.5.cloned.1.call-done = f32[128,128]{0,1:T(8,128)} async-done(((f32[128,128]{0,1:T(8,128)}), f32[128,128]{0,1:T(8,128)}) %all-reduce.5.cloned.1.call-update) | async-done | bytes 65552 | tf_op jit(solution)/shard_map/psum | solution.py:24
  73.6 1.8 fusion.11
  75.4 0.0 all-reduce.7.cloned.1.call-update
  75.4 0.2 all-reduce.9.cloned.1.call-start
  75.6 174.4 %all-reduce.7.cloned.1.call-done = f32[128,128]{0,1:T(8,128)} async-done(((f32[128,128]{0,1:T(8,128)}), f32[128,128]{0,1:T(8,128)}) %all-reduce.7.cloned.1.call-update) | async-done | bytes 65552 | tf_op jit(solution)/shard_map/psum | solution.py:25
  250.1 0.9 copy.14
  251.0 0.9 fusion.10
  251.9 11.7 %cholesky.16 = f32[128,128]{1,0:T(8,128)S(1)} custom-call(f32[128,128]{1,0:T(8,128)S(1)} %fusion.10), custom_call_target="Cholesky" | custom-call | tf_op jit(solution)/shard_map/jit(cholesky)/cholesky | solution.py:28
  263.6 0.6 compare_reduce_fusion
  264.2 0.7 fusion.7
  264.9 9.8 %custom-call.6 = f32[1,128,128]{1,2,0:T(8,128)S(1)} custom-call(f32[1,128,128]{2,1,0:T(8,128)S(1)} %fusion.7), custom_call_target="InvertDiagBlocksLowerTriangular" | custom-call | tf_op jit(solution)/shard_map/triangular_solve | solution.py:29
  274.7 1.1 fusion.8
  275.9 0.0 copy-start
  275.9 12.1 %fusion.12 = f32[128,16384]{1,0:T(8,128)} fusion(f32[128,128]{1,0:T(8,128)S(1)} %fusion.8, f32[128,16384]{0,1:T(8,128)} %bitcast.28), kind=kOutput, calls=%fused_computation.22 | convolution fusion | flops 3221225472 | bytes 16842752 | tf_op jit(solution)/shard_map/dot_general | solution.py:33
  287.9 0.0 copy-done
  287.9 0.0 copy-start.4
  287.9 0.0 copy-start.2
  287.9 0.0 copy-start.3
  287.9 0.0 copy-start.1
  288.0 0.0 all-reduce.9.cloned.1.call-update
  288.0 0.6 copy-done.4
  288.6 0.6 dynamic-slice
  289.8 0.0 copy-done.2
  289.9 0.0 copy-done.3
  289.9 0.0 copy-done.1
  289.9 0.1 broadcast_multiply_fusion
  290.0 200.5 %all-reduce.9.cloned.1.call-done = f32[128,16384]{1,0:T(8,128)} async-done(((f32[128,16384]{1,0:T(8,128)}), f32[128,16384]{1,0:T(8,128)}) %all-reduce.9.cloned.1.call-update) | async-done | bytes 8388624
  490.5 1.1 constant_dynamic-slice_fusion
  491.6 0.1 reshape.68
  491.7 1.4 reshape.67
  493.1 0.6 convolution_bitcast_fusion
  493.7 7.1 %psum.23 = f32[2,8,128]{2,1,0:T(8,128)} all-reduce(f32[2,8,128]{2,1,0:T(8,128)S(1)} %convolution_bitcast_fusion), channel_id=1, replica_groups=mesh['space'=64,'pa'=2,'pb'=2] {'pb'}, use_global_device_ids=true, to_apply=%region_5.6 | all-reduce | flops 2048 | bytes 16384 | tf_op jit(solution)/shard_map/psum | solution.py:54
  (2 shorter events, 0.0 us)
Async XLA Ops:
  7.2 66.4 %all-reduce.5.cloned.1.call-start = ((), (), s32[]{:S(2)}) async-start(), calls=%async_computation | async-start | bytes 131072 | tf_op jit(solution)/shard_map/psum | solution.py:24
  25.4 224.7 %all-reduce.7.cloned.1.call-start = ((), (), s32[]{:S(2)}) async-start(), calls=%async_computation.1 | async-start | bytes 131072 | tf_op jit(solution)/shard_map/psum | solution.py:25
  75.4 415.1 %all-reduce.9.cloned.1.call-start = ((), (), s32[]{:S(2)}) async-start(), calls=%async_computation.2 | async-start | bytes 16777216
  275.9 12.1 %copy-start = (f32[128,128]{1,0:T(8,128)}, f32[128,128]{1,0:T(8,128)S(1)}, u32[]{:S(2)}) copy-start(f32[128,128]{1,0:T(8,128)S(1)} %fusion.8) | copy-start | bytes 196612
  287.9 0.7 copy-start.4
  287.9 1.9 copy-start.2
  287.9 1.9 copy-start.3
  287.9 1.9 copy-start.1
Sparse Core Ops, SparseCore 0:
  25.5 48.0 all-reduce.4
  77.6 172.3 all-reduce.6
  288.1 202.3 all-reduce.8
where the time goes:
time: 508 us; the launch traced here: 507 us
  waiting for transfers between devices  423 us (83%)
  matrix products  32.3 us (6%)
  other arithmetic  25.3 us (5%)
  between operations  14.5 us (3%)
  blocking collectives  7.1 us (1%)
    unnamed x4, waiting for transfers between devices  201 us
    psum x1, waiting for transfers between devices, body(): lax.psum(jnp.dot(sketch.T, sketch, precision=highest, preferred_element_t...  174 us
    psum x1, waiting for transfers between devices, body(): sketch = lax.psum(partial_sketch, ('pa', 'pb'))  48.2 us
    dot_general x1, matrix products, body(): jnp.dot(flat, omega, precision=highest, preferred_element_type=jnp.float32)  16.7 us
    another operation x3, other arithmetic, body(): lower = jnp.linalg.cholesky(gram)  12.4 us
    dot_general x1, matrix products, body(): lax.dot_general(basis, flat, (((0,), (0,)), ((), ())), precision=highest,...  12.1 us
    another operation x2, other arithmetic, body(): lax.linalg.triangular_solve(lower, sketch, left_side=False, lower=True, t...  10.5 us
  transfers between devices with their start and end apart: 3, of which 3 were waited for; matrix products, arithmetic and copies ran while one was open for 0% of the time, Pallas kernels for 0%

commit v1 on v0

--- a/solution.py
+++ b/solution.py
@@ -21,7 +21,7 @@
         * g_fourth[None, None, None, :, :]
     ).reshape(width, RANK)
     partial_sketch = jnp.dot(flat, omega, precision=highest, preferred_element_type=jnp.float32)
-    sketch = lax.psum(partial_sketch, ("pa", "pb"))
+    sketch = jnp.sum(lax.all_gather(partial_sketch, ("pa", "pb")), axis=0)
     gram = lax.psum(
         jnp.dot(sketch.T, sketch, precision=highest, preferred_element_type=jnp.float32), "space"
     )

time: 508 us -> 470 us (0.925)
  waiting for transfers between devices: 423 us -> 373 us
  blocking collectives: 7.1 us -> 21.8 us
    psum x1 -> x0, waiting for transfers between devices: 48.2 us -> none  [body(): sketch = lax.psum(partial_sketch, ('pa', 'pb'))]
    all_gather x0 -> x1, blocking collectives: none -> 14.7 us  [body(): sketch = jnp.sum(lax.all_gather(partial_sketch, ('pa', 'pb')), axis=0)]
    unnamed x4 -> x3, waiting for transfers between devices: 201 us -> 200 us
  transfers between devices with their start and end apart: 3 -> 2, of which waited for: 3 -> 2; matrix products, arithmetic and copies ran while one was open for 0% -> 0% of each run, Pallas kernels for 0% -> 0%
where the time goes in v1:
time: 470 us
  waiting for transfers between devices  373 us (79%)
  matrix products  29.7 us (6%)
  other arithmetic  25.4 us (5%)
  blocking collectives  21.8 us (5%)
  between operations  14.8 us (3%)
  local copies, waits for them, and re-layouts  4.81 us (1%)
    unnamed x3, waiting for transfers between devices  200 us
    psum x1, waiting for transfers between devices, body(): lax.psum(jnp.dot(sketch.T, sketch, precision=highest, preferred_element_t...  173 us
    dot_general x1, matrix products, body(): jnp.dot(flat, omega, precision=highest, preferred_element_type=jnp.float32)  16.1 us
    all_gather x1, blocking collectives, body(): sketch = jnp.sum(lax.all_gather(partial_sketch, ('pa', 'pb')), axis=0)  14.7 us
    another operation x3, other arithmetic, body(): lower = jnp.linalg.cholesky(gram)  12.4 us
    dot_general x1, matrix products, body(): lax.dot_general(basis, flat, (((0,), (0,)), ((), ())), precision=highest,...  11.8 us
    another operation x2, other arithmetic, body(): lax.linalg.triangular_solve(lower, sketch, left_side=False, lower=True, t...  10.5 us
  transfers between devices with their start and end apart: 2, of which 2 were waited for; matrix products, arithmetic and copies ran while one was open for 0% of the time, Pallas kernels for 0%

profile of v1, /device:TPU:2, one launch (start us, length us, event | category | flops | bytes accessed | tf_op | source)
XLA Modules:
  0.0 469.8 jit_solution(6710109911577811992)
XLA Ops:
  7.2 0.0 all-reduce.4.cloned.1.call-start
  7.2 0.7 broadcast_multiply_fusion.3
  7.9 0.7 broadcast_multiply_fusion.1
  8.6 16.1 %fusion.4 = f32[128,128]{0,1:T(8,128)S(1)} fusion(f32[128,8,16,8,16]{0,4,3,2,1:T(8,128)} %param.8, f32[16,128]{1,0:T(8,128)} %param.12, f32[8,16,8,128]{3,2,1,0:T(8,128)S(1)} %broadcast_multiply_fusion.1), kind=kOutput, calls=%fused_computation.4 | convolution fusion | flops 3223322624 | bytes 8986624 | tf_op jit(solution)/shard_map/dot_general | solution.py:23
  24.8 14.7 %all-gather = f32[512,128]{0,1:T(8,128)S(1)} all-gather(f32[128,128]{0,1:T(8,128)S(1)} %fusion.4), channel_id=2, replica_groups=mesh['space'=64,'pa'=2,'pb'=2] {'pa','pb'}, dimensions={0}, use_global_device_ids=true | all-gather | bytes 327680 | tf_op jit(solution)/shard_map/all_gather | solution.py:24
  39.5 0.1 reshape.70
  39.6 0.2 reduce_sum.9
  39.7 0.9 fusion.11
  40.6 0.0 all-reduce.4.cloned.1.call-update
  40.6 0.2 all-reduce.6.cloned.1.call-start
  40.9 172.6 %all-reduce.4.cloned.1.call-done = f32[128,128]{0,1:T(8,128)} async-done(((f32[128,128]{0,1:T(8,128)}), f32[128,128]{0,1:T(8,128)}) %all-reduce.4.cloned.1.call-update) | async-done | bytes 65552 | tf_op jit(solution)/shard_map/psum | solution.py:25
  213.4 0.9 copy.14
  214.4 0.9 fusion.10
  215.2 11.7 %cholesky.16 = f32[128,128]{1,0:T(8,128)S(1)} custom-call(f32[128,128]{1,0:T(8,128)S(1)} %fusion.10), custom_call_target="Cholesky" | custom-call | tf_op jit(solution)/shard_map/jit(cholesky)/cholesky | solution.py:28
  227.0 0.6 compare_reduce_fusion
  227.6 0.7 fusion.7
  228.3 9.8 %custom-call.6 = f32[1,128,128]{1,2,0:T(8,128)S(1)} custom-call(f32[1,128,128]{2,1,0:T(8,128)S(1)} %fusion.7), custom_call_target="InvertDiagBlocksLowerTriangular" | custom-call | tf_op jit(solution)/shard_map/triangular_solve | solution.py:29
  238.1 0.3 fusion.8
  238.4 0.0 copy-start
  238.4 11.8 %fusion.12 = f32[128,16384]{1,0:T(8,128)} fusion(f32[128,128]{1,0:T(8,128)S(1)} %fusion.8, f32[128,16384]{0,1:T(8,128)} %bitcast.30), kind=kOutput, calls=%fused_computation.22 | convolution fusion | flops 3221225472 | bytes 16842752 | tf_op jit(solution)/shard_map/dot_general | solution.py:33
  250.1 0.0 copy-done
  250.1 0.0 copy-start.4
  250.1 0.0 copy-start.2
  250.2 0.0 copy-start.3
  250.2 0.0 copy-start.1
  250.2 0.0 all-reduce.6.cloned.1.call-update
  250.2 0.6 copy-done.4
  250.8 0.6 dynamic-slice
  252.1 0.0 copy-done.2
  252.1 0.0 copy-done.3
  252.1 0.0 copy-done.1
  252.1 0.1 broadcast_multiply_fusion
  252.2 200.5 %all-reduce.6.cloned.1.call-done = f32[128,16384]{1,0:T(8,128)} async-done(((f32[128,16384]{1,0:T(8,128)}), f32[128,16384]{1,0:T(8,128)}) %all-reduce.6.cloned.1.call-update) | async-done | bytes 8388624
  452.7 1.1 constant_dynamic-slice_fusion
  453.8 0.1 reshape.68
  453.9 1.4 reshape.67
  455.3 0.6 convolution_bitcast_fusion
  455.9 7.1 %psum.15 = f32[2,8,128]{2,1,0:T(8,128)} all-reduce(f32[2,8,128]{2,1,0:T(8,128)S(1)} %convolution_bitcast_fusion), channel_id=1, replica_groups=mesh['space'=64,'pa'=2,'pb'=2] {'pb'}, use_global_device_ids=true, to_apply=%region_5.6 | all-reduce | flops 2048 | bytes 16384 | tf_op jit(solution)/shard_map/psum | solution.py:54
  (2 shorter events, 0.0 us)
Async XLA Ops:
  7.2 206.3 %all-reduce.4.cloned.1.call-start = ((), (), s32[]{:S(2)}) async-start(), calls=%async_computation | async-start | bytes 131072 | tf_op jit(solution)/shard_map/psum | solution.py:25
  40.6 412.1 %all-reduce.6.cloned.1.call-start = ((), (), s32[]{:S(2)}) async-start(), calls=%async_computation.1 | async-start | bytes 16777216
  238.4 11.8 %copy-start = (f32[128,128]{1,0:T(8,128)}, f32[128,128]{1,0:T(8,128)S(1)}, u32[]{:S(2)}) copy-start(f32[128,128]{1,0:T(8,128)S(1)} %fusion.8) | copy-start | bytes 196612
  250.1 0.7 copy-start.4
  250.1 1.9 copy-start.2
  250.2 1.9 copy-start.3
  250.2 1.9 copy-start.1
Sparse Core Ops, SparseCore 0:
  40.8 172.6 all-reduce.3
  250.3 202.3 all-reduce.5
